TPU v7x, 256 devices: a whole 4x4x8 slice. The times are simulated.
256 devices in a mesh: sub: 16 (over z, core), fr: 16 (over y, x).
Axes of the slice: x: 4, y: 4, z: 8, core: 2. Of those that a mesh axis runs over, the one named last changes fastest.
Arguments:
- front_leaf: bfloat16 [32768, 2048], P(('sub', 'fr')), as said below
- shares_one: float32 [32768, 384], P(('sub', 'fr')), as said below
- shares_two: float32 [32768, 384], P(('sub', 'fr')), as said below
- map_leaf: int32 [16, 13], P('sub'), may hold values from 0 to 15, as said below
- map_mid: int32 [8, 13], replicated, may hold values from 0 to 15, as said below
Outputs:
- leaf_panel: float32 [32768, 384], P(('sub', 'fr'))
- middle_panel: float32 [32768, 384], P(('sub', 'fr'))
- top_panel: float32 [32768, 384], P(('sub', 'fr'))
- contribution: float32 [32768, 1664], P(('sub', 'fr'))
Inputs may be any that keep to these rules, and one draw needn't show every extreme that they name: `front_leaf`: each block of 2048 rows is a symmetric positive definite front. `shares_one`: in each block of 2048 rows the first 384 rows are symmetric; with the extended contributions every middle front is positive definite. `shares_two`: in each block of 2048 rows the first 384 rows are symmetric; with the extended contributions every top front is positive definite. `map_leaf`: each row lists 13 different blocks; rows 2q and 2q+1 together name every block of their parent. `map_mid`: each row lists 13 different blocks; rows 2r and 2r+1 together name every block of their parent.
All inputs are finite; a program needn't handle non-finite values.
Results may differ from a plain program's by a relative error of at most 0.0003.
Values sent between devices are 32-bit elements; how exact they have to be, the bound alone decides.
No kernel may reach another device: no remote copies, remote signals or barrier semaphores. Data moves between devices by JAX's collectives and lax.ppermute only.
A program may use at most 128 MiB of HBM per device.

v0:
```python
import jax
import jax.numpy as jnp
from jax import lax
from jax.sharding import PartitionSpec as P

BLK = 128
P_SIZE = 384
NFB = 16
NPB = 3


HIGH = lax.Precision.HIGHEST


def partner(array, axis, stride):
    return lax.ppermute(array, axis, [(i, i ^ 1 << stride) for i in range(lax.axis_size(axis))])


def eliminate(front, row_start):
    row_count, front_order = front.shape
    panels = []
    for block_index in range(NPB):
        block_low = block_index * BLK
        gathered = lax.all_gather(front[:, block_low : block_low + BLK], "fr", axis=0, tiled=True)
        row_ids = jnp.arange(front_order)
        lower_block = jnp.linalg.cholesky(gathered[block_low : block_low + BLK])
        solved = lax.linalg.triangular_solve(
            lower_block, gathered, left_side=False, lower=True, transpose_a=True
        )
        below = jnp.where((row_ids >= block_low + BLK)[:, None], solved, 0.0)
        placed = below.at[block_low : block_low + BLK].set(lower_block)
        own_below = lax.dynamic_slice_in_dim(below, row_start, row_count, 0)
        own_panel = lax.dynamic_slice_in_dim(placed, row_start, row_count, 0)
        front = front - jnp.dot(
            own_below, below.T, precision=HIGH, preferred_element_type=jnp.float32
        )
        panels.append(own_panel)
    return (jnp.concatenate(panels, axis=1), front)


def make_table(block_map):
    padded = jnp.concatenate([jnp.full((NPB,), -1, jnp.int32), block_map])
    return (padded[:, None] == jnp.arange(NFB, dtype=jnp.int32)[None, :]).astype(jnp.float32)


def extend(front, block_map, row_start):
    row_count, front_order = front.shape
    block_share = row_count // BLK
    block_table = make_table(block_map)
    padded = jnp.concatenate([jnp.full((NPB,), -1, jnp.int32), block_map])
    parents = row_start // BLK + jnp.arange(block_share)
    matches = padded[None, :] == parents[:, None]
    present = jnp.any(matches, axis=1)
    source_block = jnp.sum(jnp.where(matches, jnp.arange(NFB)[None, :], 0), axis=1)
    source_rows = (source_block[:, None] * BLK + jnp.arange(BLK)[None, :]).reshape(row_count)
    is_live = jnp.repeat(present, BLK)
    shard_rows = lax.all_gather(front, "fr", axis=0, tiled=True)
    inside = is_live & (source_rows >= 0) & (source_rows < shard_rows.shape[0])
    picked_rows = jnp.take(shard_rows, jnp.clip(source_rows, 0, shard_rows.shape[0] - 1), axis=0)
    picked_rows = jnp.where(inside[:, None], picked_rows, 0.0)
    mapped = jnp.einsum(
        "rqc,qe->rec", picked_rows.reshape(row_count, NFB, BLK), block_table, precision=HIGH
    )
    return mapped.reshape(row_count, front_order)


def combine(front, shares, block_map, row_start, level_bit):
    front_order = front.shape[1]
    piece_part = extend(front, block_map, row_start) + jnp.pad(
        shares, ((0, 0), (0, front_order - P_SIZE))
    )
    return piece_part + partner(piece_part, "sub", level_bit)


def local(front_leaf, shares_one, shares_two, map_leaf, map_mid):
    row_count = front_leaf.shape[0]
    row_start = lax.axis_index("fr") * row_count
    sub_index = lax.axis_index("sub")
    leaf_panel, child_front = eliminate(front_leaf.astype(jnp.float32), row_start)
    shares_sum = shares_two + partner(shares_two, "sub", 0)
    middle_front = combine(child_front, shares_one, map_leaf[0], row_start, 0)
    middle_panel, middle_front = eliminate(middle_front, row_start)
    pair_map = lax.dynamic_index_in_dim(map_mid, sub_index // 2, 0, keepdims=False)
    top_front = combine(middle_front, shares_sum, pair_map, row_start, 1)
    top_panel, top_front = eliminate(top_front, row_start)
    row_ids = row_start + jnp.arange(row_count)
    contribution = jnp.where((row_ids >= P_SIZE)[:, None], top_front[:, P_SIZE:], 0.0)
    return (leaf_panel, middle_panel, top_panel, contribution)


def solution(mesh):
    in_specs = (
        P(("sub", "fr"), None),
        P(("sub", "fr"), None),
        P(("sub", "fr"), None),
        P("sub", None),
        P(),
    )
    out_specs = (
        P(("sub", "fr"), None),
        P(("sub", "fr"), None),
        P(("sub", "fr"), None),
        P(("sub", "fr"), None),
    )
    return jax.shard_map(local, mesh=mesh, in_specs=in_specs, out_specs=out_specs, check_vma=False)
```

profile of v0, /device:TPU:2, one launch (start us, length us, event | category | flops | bytes accessed | tf_op | source)
XLA Modules:
  0.0 1077.1 jit_solution(2914424873114445792)
XLA Ops:
  9.3 52.5 %all-gather.12.cloned.1.call-done = f32[2048,128]{0,1:T(8,128)} async-done(((f32[128,128]{0,1:T(8,128)}), f32[2048,128]{0,1:T(8,128)}) %all-gather.12.cloned.1.call-update) | async-done | bytes 1048592 | tf_op jit(solution)/shard_map/all_gather | solution.py:24
  63.6 11.7 %cholesky.149 = f32[128,128]{1,0:T(8,128)S(1)} custom-call(f32[128,128]{1,0:T(8,128)S(1)} %fusion.29), custom_call_target="Cholesky" | custom-call | tf_op jit(solution)/shard_map/jit(cholesky)/cholesky | solution.py:26
  76.6 9.8 custom-call.13
  86.5 2.3 fusion.8
  91.5 47.4 %all-gather.14.cloned.1.call-done = f32[2048,128]{0,1:T(8,128)} async-done(((f32[128,128]{0,1:T(8,128)}), f32[2048,128]{0,1:T(8,128)}) %all-gather.14.cloned.1.call-update) | async-done | bytes 1048592 | tf_op jit(solution)/shard_map/all_gather | solution.py:24
  140.7 11.7 %cholesky.160 = f32[128,128]{1,0:T(8,128)S(1)} custom-call(f32[128,128]{1,0:T(8,128)S(1)} %fusion.27), custom_call_target="Cholesky" | custom-call | tf_op jit(solution)/shard_map/jit(cholesky)/cholesky | solution.py:26
  153.8 9.8 custom-call.14
  163.6 2.3 fusion.7
  169.8 47.2 %all-gather.16.cloned.1.call-done = f32[2048,128]{0,1:T(8,128)} async-done(((f32[128,128]{0,1:T(8,128)}), f32[2048,128]{0,1:T(8,128)}) %all-gather.16.cloned.1.call-update) | async-done | bytes 1048592 | tf_op jit(solution)/shard_map/all_gather | solution.py:24
  218.8 11.7 %cholesky.171 = f32[128,128]{1,0:T(8,128)S(1)} custom-call(f32[128,128]{1,0:T(8,128)S(1)} %fusion.25), custom_call_target="Cholesky" | custom-call | tf_op jit(solution)/shard_map/jit(cholesky)/cholesky | solution.py:26
  231.9 9.8 custom-call.15
  241.7 2.3 fusion.6
  244.9 4.0 convolution_subtract_fusion.5
  255.3 118.1 %all-gather.18.cloned.1.call-done = f32[2048,2048]{0,1:T(8,128)} async-done(((f32[128,2048]{0,1:T(8,128)}), f32[2048,2048]{0,1:T(8,128)}) %all-gather.18.cloned.1.call-update) | async-done | bytes 16777232 | tf_op jit(solution)/shard_map/all_gather | solution.py:57
  373.4 17.6 %copy.19 = f32[2048,2048]{1,0:T(8,128)} copy(f32[2048,2048]{0,1:T(8,128)} %all-gather.18.cloned.1.call-done) | data formatting | bytes 33554432 | tf_op jit(solution)/shard_map/all_gather | solution.py:57
  391.0 7.3 gather_fusion
  403.6 2.6 collective-permute-done
  407.0 47.7 %all-gather.20.cloned.1.call-done = f32[2048,128]{0,1:T(8,128)} async-done(((f32[128,128]{0,1:T(8,128)}), f32[2048,128]{0,1:T(8,128)}) %all-gather.20.cloned.1.call-update) | async-done | bytes 1048592 | tf_op jit(solution)/shard_map/all_gather | solution.py:24
  456.5 11.7 %cholesky.182 = f32[128,128]{1,0:T(8,128)S(1)} custom-call(f32[128,128]{1,0:T(8,128)S(1)} %fusion.23), custom_call_target="Cholesky" | custom-call | tf_op jit(solution)/shard_map/jit(cholesky)/cholesky | solution.py:26
  470.2 9.8 custom-call.16
  480.0 2.3 fusion.5
  486.0 47.4 %all-gather.22.cloned.1.call-done = f32[2048,128]{0,1:T(8,128)} async-done(((f32[128,128]{0,1:T(8,128)}), f32[2048,128]{0,1:T(8,128)}) %all-gather.22.cloned.1.call-update) | async-done | bytes 1048592 | tf_op jit(solution)/shard_map/all_gather | solution.py:24
  535.2 11.7 %cholesky.193 = f32[128,128]{1,0:T(8,128)S(1)} custom-call(f32[128,128]{1,0:T(8,128)S(1)} %fusion.21), custom_call_target="Cholesky" | custom-call | tf_op jit(solution)/shard_map/jit(cholesky)/cholesky | solution.py:26
  548.9 9.8 custom-call.17
  558.7 2.3 fusion.4
  562.0 3.0 convolution_subtract_fusion.3
  566.1 47.2 %all-gather.24.cloned.1.call-done = f32[2048,128]{0,1:T(8,128)} async-done(((f32[128,128]{0,1:T(8,128)}), f32[2048,128]{0,1:T(8,128)}) %all-gather.24.cloned.1.call-update) | async-done | bytes 1048592 | tf_op jit(solution)/shard_map/all_gather | solution.py:24
  615.2 11.7 %cholesky.204 = f32[128,128]{1,0:T(8,128)S(1)} custom-call(f32[128,128]{1,0:T(8,128)S(1)} %fusion.19), custom_call_target="Cholesky" | custom-call | tf_op jit(solution)/shard_map/jit(cholesky)/cholesky | solution.py:26
  628.8 9.8 custom-call.18
  638.7 2.3 fusion.3
  641.9 2.8 convolution_subtract_fusion.2
  650.6 118.5 %all-gather.26.cloned.1.call-done = f32[2048,2048]{0,1:T(8,128)} async-done(((f32[128,2048]{0,1:T(8,128)}), f32[2048,2048]{0,1:T(8,128)}) %all-gather.26.cloned.1.call-update) | async-done | bytes 16777232 | tf_op jit(solution)/shard_map/all_gather | solution.py:57
  769.2 17.6 %copy.31 = f32[2048,2048]{1,0:T(8,128)} copy(f32[2048,2048]{0,1:T(8,128)} %all-gather.26.cloned.1.call-done) | data formatting | bytes 33554432 | tf_op jit(solution)/shard_map/all_gather | solution.py:57
  786.8 7.3 gather_fusion.1
  800.9 22.0 %collective-permute-done.2 = f32[128,2048]{0,1:T(8,128)S(1)} collective-permute-done((f32[128,2048]{0,1:T(8,128)S(1)}, f32[128,2048]{0,1:T(8,128)S(1)}, u32[]{:S(2)}, u32[]{:S(2)}) %collective-permute-start.2) | collective-permute-done | bytes 1048608 | tf_op jit(solution)/shard_map/ppermute | solution.py:16
  823.7 47.7 %all-gather.28.cloned.1.call-done = f32[2048,128]{0,1:T(8,128)} async-done(((f32[128,128]{0,1:T(8,128)}), f32[2048,128]{0,1:T(8,128)}) %all-gather.28.cloned.1.call-update) | async-done | bytes 1048592 | tf_op jit(solution)/shard_map/all_gather | solution.py:24
  875.9 13.2 %cholesky.215 = f32[128,128]{1,0:T(8,128)} custom-call(f32[128,128]{1,0:T(8,128)} %fusion.17), custom_call_target="Cholesky" | custom-call | tf_op jit(solution)/shard_map/jit(cholesky)/cholesky | solution.py:26
  892.8 11.3 %custom-call.19 = f32[1,128,128]{1,2,0:T(8,128)} custom-call(f32[1,128,128]{2,1,0:T(8,128)} %get-tuple-element.123), custom_call_target="InvertDiagBlocksLowerTriangular" | custom-call | tf_op jit(solution)/shard_map/triangular_solve/custom-call.0 | solution.py:27
  904.1 2.3 fusion.2
  910.9 46.7 %all-gather.30.cloned.1.call-done = f32[2048,128]{0,1:T(8,128)} async-done(((f32[128,128]{0,1:T(8,128)}), f32[2048,128]{0,1:T(8,128)}) %all-gather.30.cloned.1.call-update) | async-done | bytes 1048592 | tf_op jit(solution)/shard_map/all_gather | solution.py:24
  959.4 11.7 %cholesky.226 = f32[128,128]{1,0:T(8,128)S(1)} custom-call(f32[128,128]{1,0:T(8,128)S(1)} %fusion.15), custom_call_target="Cholesky" | custom-call | tf_op jit(solution)/shard_map/jit(cholesky)/cholesky | solution.py:26
  972.5 10.4 custom-call.20
  982.9 2.3 fusion.1
  985.2 3.0 convolution_subtract_fusion
  1003.0 34.7 %all-gather.32.cloned.1.call-done = f32[2048,128]{0,1:T(8,128)} async-done(((f32[128,128]{0,1:T(8,128)}), f32[2048,128]{0,1:T(8,128)}) %all-gather.32.cloned.1.call-update) | async-done | bytes 1048592 | tf_op jit(solution)/shard_map/all_gather | solution.py:24
  1039.4 11.9 %cholesky.237 = f32[128,128]{1,0:T(8,128)S(1)} custom-call(f32[128,128]{1,0:T(8,128)S(1)} %fusion.13), custom_call_target="Cholesky" | custom-call | tf_op jit(solution)/shard_map/jit(cholesky)/cholesky | solution.py:26
  1052.7 9.8 custom-call.21
  1062.5 2.3 fusion
  (188 shorter events, 100.2 us)
Async XLA Ops:
  7.2 639.0 %copy-start = (s32[8,13]{1,0:T(8,128)S(1)}, s32[8,13]{1,0:T(8,128)}, u32[]{:S(2)}) copy-start(s32[8,13]{1,0:T(8,128)} %param.32) | copy-start | bytes 1252
  7.2 242.1 %copy-start.13 = (s32[1,13]{1,0:T(1,128)S(1)}, s32[1,13]{1,0:T(1,128)}, u32[]{:S(2)}) copy-start(s32[1,13]{1,0:T(1,128)} %param.31) | copy-start | bytes 160
  7.2 54.6 %all-gather.12.cloned.1.call-start = ((), (), s32[]{:S(2)}) async-start(), calls=%async_computation | async-start | bytes 1114112 | tf_op jit(solution)/shard_map/all_gather | solution.py:24
  9.2 129.7 %all-gather.14.cloned.1.call-start = ((), (), s32[]{:S(2)}) async-start(), calls=%async_computation.1 | async-start | bytes 1114112 | tf_op jit(solution)/shard_map/all_gather | solution.py:24
  91.2 125.8 %all-gather.16.cloned.1.call-start = ((), (), s32[]{:S(2)}) async-start(), calls=%async_computation.2 | async-start | bytes 1114112 | tf_op jit(solution)/shard_map/all_gather | solution.py:24
  167.7 1.0 copy-start.7
  169.3 204.1 %all-gather.18.cloned.1.call-start = ((), (), s32[]{:S(2)}) async-start(), calls=%async_computation.3 | async-start | bytes 17825792 | tf_op jit(solution)/shard_map/all_gather | solution.py:57
  243.9 1.0 copy-start.1
  249.0 205.7 %all-gather.20.cloned.1.call-start = ((), (), s32[]{:S(2)}) async-start(), calls=%async_computation.4 | async-start | bytes 1114112 | tf_op jit(solution)/shard_map/all_gather | solution.py:24
  403.5 2.7 collective-permute-start
  407.0 126.4 %all-gather.22.cloned.1.call-start = ((), (), s32[]{:S(2)}) async-start(), calls=%async_computation.5 | async-start | bytes 1114112 | tf_op jit(solution)/shard_map/all_gather | solution.py:24
  482.2 1.8 copy-start.2
  484.1 1.0 copy-start.8
  485.7 127.6 %all-gather.24.cloned.1.call-start = ((), (), s32[]{:S(2)}) async-start(), calls=%async_computation.6 | async-start | bytes 1114112 | tf_op jit(solution)/shard_map/all_gather | solution.py:24
  561.0 1.0 copy-start.3
  565.7 203.5 %all-gather.26.cloned.1.call-start = ((), (), s32[]{:S(2)}) async-start(), calls=%async_computation.7 | async-start | bytes 17825792 | tf_op jit(solution)/shard_map/all_gather | solution.py:57
  640.9 1.0 copy-start.4
  644.8 226.6 %all-gather.28.cloned.1.call-start = ((), (), s32[]{:S(2)}) async-start(), calls=%async_computation.8 | async-start | bytes 1114112 | tf_op jit(solution)/shard_map/all_gather | solution.py:24
  645.9 4.7 collective-permute-start.1
  799.2 195.6 %copy-start.10 = (f32[128,128]{1,0:T(8,128)S(1)}, f32[128,128]{1,0:T(8,128)}, u32[]{:S(2)}) copy-start(f32[128,128]{1,0:T(8,128)} %get-tuple-element.130) | copy-start | bytes 196612
  799.3 197.1 %copy-start.11 = (f32[128,128]{1,0:T(8,128)S(1)}, f32[128,128]{1,0:T(8,128)}, u32[]{:S(2)}) copy-start(f32[128,128]{1,0:T(8,128)} %get-tuple-element.128) | copy-start | bytes 196612
  799.3 198.7 %copy-start.12 = (f32[128,128]{1,0:T(8,128)S(1)}, f32[128,128]{1,0:T(8,128)}, u32[]{:S(2)}) copy-start(f32[128,128]{1,0:T(8,128)} %get-tuple-element.126) | copy-start | bytes 196612
  799.3 23.6 %collective-permute-start.2 = (f32[128,2048]{0,1:T(8,128)S(1)}, f32[128,2048]{0,1:T(8,128)S(1)}, u32[]{:S(2)}, u32[]{:S(2)}) collective-permute-start(f32[128,2048]{0,1:T(8,128)S(1)} %bitcast_add_fusion), channel_id=1, source_target_pairs={{0,32},{16,48},{32,0},{48,16},{64,96},{80,112},{96,64},{112,80},{1... | collective-permute-start | bytes 3145736 | tf_op jit(solution)/shard_map/ppermute | solution.py:16
  823.7 133.9 %all-gather.30.cloned.1.call-start = ((), (), s32[]{:S(2)}) async-start(), calls=%async_computation.9 | async-start | bytes 1114112 | tf_op jit(solution)/shard_map/all_gather | solution.py:24
  906.4 1.8 copy-start.5
  908.2 1.0 copy-start.6
  909.9 127.7 %all-gather.32.cloned.1.call-start = ((), (), s32[]{:S(2)}) async-start(), calls=%async_computation.10 | async-start | bytes 1114112 | tf_op jit(solution)/shard_map/all_gather | solution.py:24
  988.2 1.0 copy-start.9
Sparse Core Ops, SparseCore 0:
  11.0 50.7 all-gather.11
  91.3 47.5 all-gather.13
  169.4 47.5 all-gather.15
  249.1 124.2 all-gather.17
  407.1 47.5 all-gather.19
  485.9 47.5 all-gather.21
  565.8 47.5 all-gather.23
  644.9 124.2 all-gather.25
  823.8 47.5 all-gather.27
  910.0 47.5 all-gather.29
  990.1 47.5 all-gather.31
where the time goes:
time: 1090 us; the launch traced here: 1080 us
  waiting for transfers between devices  680 us (62%)
  other arithmetic  237 us (22%)
  local copies, waits for them, and re-layouts  94.7 us (9%)
  matrix products  44.9 us (4%)
  between operations  16.4 us (2%)
    all_gather x9, waiting for transfers between devices, eliminate(): lax.all_gather(front[:, block_low:block_low + BLK], 'fr', axis=0, tiled=T...  419 us
    all_gather x2, waiting for transfers between devices, extend(): shard_rows = lax.all_gather(front, 'fr', axis=0, tiled=True)  237 us
    another operation x27, other arithmetic, eliminate(): lower_block = jnp.linalg.cholesky(gathered[block_low:block_low + BLK])  114 us
    another operation x18, other arithmetic, eliminate(): lax.linalg.triangular_solve(lower_block, gathered, left_side=False, lower...  99.7 us
    all_gather x2, local copies, waits for them, and re-layouts, extend(): shard_rows = lax.all_gather(front, 'fr', axis=0, tiled=True)  35.2 us
    ppermute x3, waiting for transfers between devices, partner(): lax.ppermute(array, axis, [(i, i ^ 1 << stride) for i in range(lax.axis_s...  24.6 us
    dot_general x9, matrix products, eliminate(): jnp.dot(own_below, below.T, precision=HIGH, preferred_element_type=jnp.fl...  22 us
  transfers between devices with their start and end apart: 14, of which 13 were waited for; matrix products, arithmetic and copies ran while one was open for 2% of the time, Pallas kernels for 0%

commit v1 on v0

v1 whole, which is shorter than its diff:
```python
import jax
import jax.numpy as jnp
from jax import lax
from jax.sharding import PartitionSpec as P

BLK = 128
P_SIZE = 384
NFB = 16
NPB = 3


HIGH = lax.Precision.HIGHEST


def partner(array, axis, stride):
    return lax.ppermute(array, axis, [(i, i ^ 1 << stride) for i in range(lax.axis_size(axis))])


def factor(columns):
    lower_block = jnp.tril(jnp.linalg.cholesky(columns[:P_SIZE]))
    solved = lax.linalg.triangular_solve(
        lower_block, columns[P_SIZE:], left_side=False, lower=True, transpose_a=True
    )
    return jnp.concatenate([lower_block, solved], axis=0)


def gather_rows(array):
    return lax.all_gather(array, "fr", axis=0, tiled=True)


def extend(rest, panel, block_map):
    parent_block = lax.axis_index("fr")
    matches = block_map == parent_block
    present = jnp.any(matches)
    child_block = NPB + jnp.argmax(matches)
    rows = lax.dynamic_slice_in_dim(rest, child_block * BLK, BLK, 0)
    panel_rows = lax.dynamic_slice_in_dim(panel, child_block * BLK, BLK, 0)
    schur = rows - jnp.dot(
        panel_rows, panel[P_SIZE:].T, precision=HIGH, preferred_element_type=jnp.float32
    )
    column_match = block_map[None, :] == jnp.arange(NFB, dtype=jnp.int32)[:, None]
    has_column = jnp.any(column_match, axis=1)
    source_column = jnp.argmax(column_match, axis=1)
    tiles = schur.reshape(BLK, NFB - NPB, BLK)
    placed = jnp.take(tiles, source_column, axis=1)
    placed = jnp.where(has_column[None, :, None] & present, placed, 0.0)
    return placed.reshape(BLK, NFB * BLK)


def level(front, row_start):
    panel = factor(gather_rows(front[:, :P_SIZE]))
    own_panel = lax.dynamic_slice_in_dim(panel, row_start, front.shape[0], 0)
    return panel, own_panel


def combine(front, shares, block_map, level_bit):
    row_start = lax.axis_index("fr") * front.shape[0]
    panel, own_panel = level(front, row_start)
    rest = gather_rows(front[:, P_SIZE:])
    piece = extend(rest, panel, block_map)
    piece = piece.at[:, :P_SIZE].add(shares)
    return own_panel, piece + partner(piece, "sub", level_bit)


def local(front_leaf, shares_one, shares_two, map_leaf, map_mid):
    row_count = front_leaf.shape[0]
    row_start = lax.axis_index("fr") * row_count
    sub_index = lax.axis_index("sub")
    shares_sum = shares_two + partner(shares_two, "sub", 0)
    leaf_panel, middle_front = combine(front_leaf.astype(jnp.float32), shares_one, map_leaf[0], 0)
    pair_map = lax.dynamic_index_in_dim(map_mid, sub_index // 2, 0, keepdims=False)
    middle_panel, top_front = combine(middle_front, shares_sum, pair_map, 1)
    panel, top_panel = level(top_front, row_start)
    schur = top_front[:, P_SIZE:] - jnp.dot(
        top_panel, panel[P_SIZE:].T, precision=HIGH, preferred_element_type=jnp.float32
    )
    row_ids = row_start + jnp.arange(row_count)
    contribution = jnp.where((row_ids >= P_SIZE)[:, None], schur, 0.0)
    return (leaf_panel, middle_panel, top_panel, contribution)


def solution(mesh):
    in_specs = (
        P(("sub", "fr"), None),
        P(("sub", "fr"), None),
        P(("sub", "fr"), None),
        P("sub", None),
        P(),
    )
    out_specs = (
        P(("sub", "fr"), None),
        P(("sub", "fr"), None),
        P(("sub", "fr"), None),
        P(("sub", "fr"), None),
    )
    return jax.shard_map(local, mesh=mesh, in_specs=in_specs, out_specs=out_specs, check_vma=False)
```

time: 1090 us -> 583 us (0.53)
  waiting for transfers between devices: 680 us -> 188 us
  local copies, waits for them, and re-layouts: 94.7 us -> 39 us
  other arithmetic: 237 us -> 278 us
    all_gather x11 -> x5, waiting for transfers between devices: 655 us -> 163 us  [gather_rows(): return lax.all_gather(array, 'fr', axis=0, tiled=True)]
    another operation x45 -> x44, other arithmetic: 214 us -> 263 us  [the longest x32 170 us: factor(): lower_block = jnp.tril(jnp.linalg.cholesky(columns[:P_SIZE]))]
    all_gather x2 -> x0, local copies, waits for them, and re-layouts: 35.2 us -> none  [extend(): shard_rows = lax.all_gather(front, 'fr', axis=0, tiled=True)]
    another operation x0 -> x40, local copies, waits for them, and re-layouts: none -> 17.9 us  [the longest x31 17.7 us: factor(): lax.linalg.triangular_solve(lower_block, columns[P_SIZE:], left_side=Fals...]
    gather x2, local copies, waits for them, and re-layouts: 14.7 us -> 1.23 us  [extend(): placed = jnp.take(tiles, source_column, axis=1)]
    dot_general x11 -> x3, matrix products: 24.5 us -> 16.4 us  [the longest x2 11 us: extend(): jnp.dot(panel_rows, panel[P_SIZE:].T, precision=HIGH, preferred_element_t...]
    another operation x9 -> x27, matrix products: 20.4 us -> 27.7 us  [the longest x15 24.6 us: factor(): lax.linalg.triangular_solve(lower_block, columns[P_SIZE:], left_side=Fals...]
  transfers between devices with their start and end apart: 14 -> 8, of which waited for: 13 -> 7; matrix products, arithmetic and copies ran while one was open for 2% -> 41% of each run, Pallas kernels for 0% -> 0%
where the time goes in v1:
time: 583 us; the launch traced here: 573 us
  other arithmetic  278 us (48%)
  waiting for transfers between devices  188 us (32%)
  matrix products  44.1 us (8%)
  local copies, waits for them, and re-layouts  39 us (7%)
  between operations  21.8 us (4%)
    another operation x32, other arithmetic, factor(): lower_block = jnp.tril(jnp.linalg.cholesky(columns[:P_SIZE]))  170 us
    all_gather x5, waiting for transfers between devices, gather_rows(): return lax.all_gather(array, 'fr', axis=0, tiled=True)  163 us
    another operation x7, other arithmetic, factor(): lax.linalg.triangular_solve(lower_block, columns[P_SIZE:], left_side=Fals...  89.5 us
    ppermute x3, waiting for transfers between devices, partner(): lax.ppermute(array, axis, [(i, i ^ 1 << stride) for i in range(lax.axis_s...  24.9 us
    another operation x15, matrix products, factor(): lax.linalg.triangular_solve(lower_block, columns[P_SIZE:], left_side=Fals...  24.6 us
    another operation x31, local copies, waits for them, and re-layouts, factor(): lax.linalg.triangular_solve(lower_block, columns[P_SIZE:], left_side=Fals...  17.7 us
  transfers between devices with their start and end apart: 8, of which 7 were waited for; matrix products, arithmetic and copies ran while one was open for 41% of the time, Pallas kernels for 0%

profile of v1, /device:TPU:2, one launch (start us, length us, event | category | flops | bytes accessed | tf_op | source)
XLA Modules:
  0.0 572.6 jit_solution(2634694661818319747)
XLA Ops:
  14.2 1.4 compare_reduce_fusion.11
  18.3 52.2 %all-gather.6.cloned.1.call-done = f32[2048,384]{0,1:T(8,128)} async-done(((f32[128,384]{0,1:T(8,128)}), f32[2048,384]{0,1:T(8,128)}) %all-gather.6.cloned.1.call-update) | async-done | bytes 3145744 | tf_op jit(solution)/shard_map/all_gather | solution.py:28
  73.0 11.7 %cholesky.273 = f32[128,128]{1,0:T(8,128)S(1)} custom-call(f32[128,128]{1,0:T(8,128)S(1)} %cholesky.428), custom_call_target="Cholesky" | custom-call | tf_op jit(solution)/shard_map/jit(cholesky)/cholesky | solution.py:20
  84.8 9.8 %custom-call.23 = f32[1,128,128]{1,2,0:T(8,128)S(1)} custom-call(f32[1,128,128]{2,1,0:T(8,128)S(1)} %get-tuple-element.128), custom_call_target="InvertDiagBlocksLowerTriangular" | custom-call | tf_op jit(solution)/shard_map/jit(cholesky)/cholesky | solution.py:20
  95.2 11.7 %cholesky.292 = f32[128,128]{1,0:T(8,128)S(1)} custom-call(f32[128,128]{1,0:T(8,128)S(1)} %cholesky.432), custom_call_target="Cholesky" | custom-call | tf_op jit(solution)/shard_map/jit(cholesky)/cholesky | solution.py:20
  106.9 10.0 %custom-call.24 = f32[1,128,128]{1,2,0:T(8,128)S(1)} custom-call(f32[1,128,128]{2,1,0:T(8,128)S(1)} %get-tuple-element.125), custom_call_target="InvertDiagBlocksLowerTriangular" | custom-call | tf_op jit(solution)/shard_map/jit(cholesky)/cholesky | solution.py:20
  117.4 11.7 %cholesky.311 = f32[128,128]{1,0:T(8,128)S(1)} custom-call(f32[128,128]{1,0:T(8,128)S(1)} %convolution_subtract_fusion.7), custom_call_target="Cholesky" | custom-call | tf_op jit(solution)/shard_map/jit(cholesky)/cholesky | solution.py:20
  132.4 5.7 %while.8 = (s32[]{:T(128)}, f32[384,384]{1,0:T(8,128)S(1)}, s32[3,2]{0,1:T(2,128)S(1)}, f32[3,128,128]{2,1,0:T(8,128)S(1)}, s32[]{:T(128)}) while((s32[]{:T(128)}, f32[384,384]{1,0:T(8,128)S(1)}, s32[3,2]{0,1:T(2,128)S(1)}, f32[3,128,128]{2,1,0:T(8,128)S(1)}, s32[]{:T(128)}) %tuple.92), condition=%wide.while_cond.2, body=%wide.while_body.2.sunk | while | flops 2 | bytes 131189 | solution.py:21
  138.2 29.9 %custom-call.25 = f32[3,128,128]{1,2,0:T(8,128)S(1)} custom-call(f32[3,128,128]{2,1,0:T(8,128)S(1)} %get-tuple-element.59), custom_call_target="InvertDiagBlocksLowerTriangular" | custom-call | tf_op jit(solution)/shard_map/triangular_solve/custom-call.2 | solution.py:21
  168.3 2.1 fusion.41
  170.4 2.1 convolution_subtract_fusion.1
  173.4 2.3 convolution_subtract_fusion
  176.6 2.1 maximum_maximum_fusion
  178.6 3.3 all-gather.8.cloned.1.call-done
  181.9 5.5 fusion.18
  189.1 2.6 collective-permute-done
  197.0 52.1 %all-gather.10.cloned.1.call-done = f32[2048,384]{0,1:T(8,128)} async-done(((f32[128,384]{0,1:T(8,128)}), f32[2048,384]{0,1:T(8,128)}) %all-gather.10.cloned.1.call-update) | async-done | bytes 3145744 | tf_op jit(solution)/shard_map/all_gather | solution.py:28
  251.5 11.7 %cholesky.326 = f32[128,128]{1,0:T(8,128)S(1)} custom-call(f32[128,128]{1,0:T(8,128)S(1)} %cholesky.436), custom_call_target="Cholesky" | custom-call | tf_op jit(solution)/shard_map/jit(cholesky)/cholesky | solution.py:20
  263.3 9.8 %custom-call.26 = f32[1,128,128]{1,2,0:T(8,128)S(1)} custom-call(f32[1,128,128]{2,1,0:T(8,128)S(1)} %get-tuple-element.121), custom_call_target="InvertDiagBlocksLowerTriangular" | custom-call | tf_op jit(solution)/shard_map/jit(cholesky)/cholesky | solution.py:20
  273.7 11.7 %cholesky.345 = f32[128,128]{1,0:T(8,128)S(1)} custom-call(f32[128,128]{1,0:T(8,128)S(1)} %cholesky.440), custom_call_target="Cholesky" | custom-call | tf_op jit(solution)/shard_map/jit(cholesky)/cholesky | solution.py:20
  285.5 10.0 %custom-call.27 = f32[1,128,128]{1,2,0:T(8,128)S(1)} custom-call(f32[1,128,128]{2,1,0:T(8,128)S(1)} %get-tuple-element.118), custom_call_target="InvertDiagBlocksLowerTriangular" | custom-call | tf_op jit(solution)/shard_map/jit(cholesky)/cholesky | solution.py:20
  296.0 11.7 %cholesky.364 = f32[128,128]{1,0:T(8,128)S(1)} custom-call(f32[128,128]{1,0:T(8,128)S(1)} %convolution_subtract_fusion.6), custom_call_target="Cholesky" | custom-call | tf_op jit(solution)/shard_map/jit(cholesky)/cholesky | solution.py:20
  311.7 6.1 %while.9 = (s32[]{:T(128)}, f32[384,384]{1,0:T(8,128)S(1)}, s32[3,2]{0,1:T(2,128)S(1)}, f32[3,128,128]{2,1,0:T(8,128)S(1)}, s32[]{:T(128)}) while((s32[]{:T(128)}, f32[384,384]{1,0:T(8,128)S(1)}, s32[3,2]{0,1:T(2,128)S(1)}, f32[3,128,128]{2,1,0:T(8,128)S(1)}, s32[]{:T(128)}) %tuple.111), condition=%wide.while_cond.2.clone, body=%wide.while_body.2.clone.sunk | while | flops 2 | bytes 131189 | solution.py:21
  317.8 29.9 %custom-call.28 = f32[3,128,128]{1,2,0:T(8,128)S(1)} custom-call(f32[3,128,128]{2,1,0:T(8,128)S(1)} %get-tuple-element.60), custom_call_target="InvertDiagBlocksLowerTriangular" | custom-call | tf_op jit(solution)/shard_map/triangular_solve/custom-call.2 | solution.py:21
  347.9 2.1 fusion.39
  350.9 2.1 fusion.38
  354.1 2.1 fusion.37
  356.2 2.1 maximum_maximum_fusion.1
  358.3 2.6 all-gather.12.cloned.1.call-done
  360.8 5.5 dynamic-slice_subtract_fusion
  367.2 1.8 fusion.53
  368.9 1.8 collective-permute-start.2
  370.7 22.2 %collective-permute-done.2 = f32[128,2048]{0,1:T(8,128)S(1)} collective-permute-done((f32[128,2048]{0,1:T(8,128)S(1)}, f32[128,2048]{0,1:T(8,128)S(1)}, u32[]{:S(2)}, u32[]{:S(2)}) %collective-permute-start.2) | collective-permute-done | bytes 1048608 | tf_op jit(solution)/shard_map/ppermute | solution.py:16
  398.3 52.5 %all-gather.14.cloned.1.call-done = f32[2048,384]{0,1:T(8,128)} async-done(((f32[128,384]{0,1:T(8,128)}), f32[2048,384]{0,1:T(8,128)}) %all-gather.14.cloned.1.call-update) | async-done | bytes 3145744 | tf_op jit(solution)/shard_map/all_gather | solution.py:28
  453.3 11.7 %cholesky.379 = f32[128,128]{1,0:T(8,128)S(1)} custom-call(f32[128,128]{1,0:T(8,128)S(1)} %cholesky.444), custom_call_target="Cholesky" | custom-call | tf_op jit(solution)/shard_map/jit(cholesky)/cholesky | solution.py:20
  465.1 9.8 %custom-call.29 = f32[1,128,128]{1,2,0:T(8,128)S(1)} custom-call(f32[1,128,128]{2,1,0:T(8,128)S(1)} %get-tuple-element.114), custom_call_target="InvertDiagBlocksLowerTriangular" | custom-call | tf_op jit(solution)/shard_map/jit(cholesky)/cholesky | solution.py:20
  475.5 11.7 %cholesky.398 = f32[128,128]{1,0:T(8,128)S(1)} custom-call(f32[128,128]{1,0:T(8,128)S(1)} %cholesky.448), custom_call_target="Cholesky" | custom-call | tf_op jit(solution)/shard_map/jit(cholesky)/cholesky | solution.py:20
  487.2 10.0 %custom-call.30 = f32[1,128,128]{1,2,0:T(8,128)S(1)} custom-call(f32[1,128,128]{2,1,0:T(8,128)S(1)} %get-tuple-element.111), custom_call_target="InvertDiagBlocksLowerTriangular" | custom-call | tf_op jit(solution)/shard_map/jit(cholesky)/cholesky | solution.py:20
  497.7 11.7 %cholesky.417 = f32[128,128]{1,0:T(8,128)S(1)} custom-call(f32[128,128]{1,0:T(8,128)S(1)} %convolution_subtract_fusion.5), custom_call_target="Cholesky" | custom-call | tf_op jit(solution)/shard_map/jit(cholesky)/cholesky | solution.py:20
  513.7 6.0 %while.10 = (s32[]{:T(128)}, f32[384,384]{1,0:T(8,128)S(1)}, s32[3,2]{0,1:T(2,128)S(1)}, f32[3,128,128]{2,1,0:T(8,128)S(1)}, s32[]{:T(128)}) while((s32[]{:T(128)}, f32[384,384]{1,0:T(8,128)S(1)}, s32[3,2]{0,1:T(2,128)S(1)}, f32[3,128,128]{2,1,0:T(8,128)S(1)}, s32[]{:T(128)}) %tuple.112), condition=%wide.while_cond.2.clone.1, body=%wide.while_body.2.clone.1.sunk | while | flops 2 | bytes 131189 | solution.py:21
  514.3 1.4 bitcast_dynamic-update-slice_fusion.8
  516.3 1.4 bitcast_dynamic-update-slice_fusion.8
  518.3 1.4 bitcast_dynamic-update-slice_fusion.8
  519.7 29.5 %custom-call.31 = f32[3,128,128]{1,2,0:T(8,128)S(1)} custom-call(f32[3,128,128]{2,1,0:T(8,128)S(1)} %get-tuple-element.61), custom_call_target="InvertDiagBlocksLowerTriangular" | custom-call | tf_op jit(solution)/shard_map/triangular_solve/custom-call.2 | solution.py:21
  549.2 2.0 fusion.35
  552.1 2.1 fusion.34
  555.3 2.1 fusion.33
  559.0 5.5 fusion.32
  (152 shorter events, 60.4 us)
Async XLA Ops:
  7.2 4.3 copy-start.5
  7.2 5.5 copy-start.3
  7.2 63.3 %all-gather.6.cloned.1.call-start = ((), (), s32[]{:S(2)}) async-start(), calls=%async_computation | async-start | bytes 3342336 | tf_op jit(solution)/shard_map/all_gather | solution.py:28
  9.0 172.9 %all-gather.8.cloned.1.call-start = ((), (), s32[]{:S(2)}) async-start(), calls=%async_computation.1 | async-start | bytes 14483456 | tf_op jit(solution)/shard_map/all_gather | solution.py:28
  11.4 237.7 %all-gather.10.cloned.1.call-start = ((), (), s32[]{:S(2)}) async-start(), calls=%async_computation.2 | async-start | bytes 3342336 | tf_op jit(solution)/shard_map/all_gather | solution.py:28
  187.4 0.9 copy-start.2
  189.0 4.7 copy-start.4
  189.0 2.7 collective-permute-start
  192.6 168.2 %all-gather.12.cloned.1.call-start = ((), (), s32[]{:S(2)}) async-start(), calls=%async_computation.3 | async-start | bytes 14483456 | tf_op jit(solution)/shard_map/all_gather | solution.py:28
  193.6 257.2 %all-gather.14.cloned.1.call-start = ((), (), s32[]{:S(2)}) async-start(), calls=%async_computation.4 | async-start | bytes 3342336 | tf_op jit(solution)/shard_map/all_gather | solution.py:28
  194.5 172.7 %collective-permute-start.1 = (f32[128,384]{0,1:T(8,128)}, f32[128,384]{0,1:T(8,128)}, u32[]{:S(2)}, u32[]{:S(2)}) collective-permute-start(f32[128,384]{0,1:T(8,128)} %copy.35), channel_id=1, source_target_pairs={{0,16},{16,0},{32,48},{48,32},{64,80},{80,64},{96,112},{112,96},{1... | collective-permute-start | bytes 589832 | tf_op jit(solution)/shard_map/ppermute | solution.py:16
  368.9 24.0 %collective-permute-start.2 = (f32[128,2048]{0,1:T(8,128)S(1)}, f32[128,2048]{0,1:T(8,128)S(1)}, u32[]{:S(2)}, u32[]{:S(2)}) collective-permute-start(f32[128,2048]{0,1:T(8,128)S(1)} %fusion.53), channel_id=1, source_target_pairs={{0,32},{16,48},{32,0},{48,16},{64,96},{80,112},{96,64},{112,80},{1... | collective-permute-start | bytes 3145736 | tf_op jit(solution)/shard_map/ppermute | solution.py:16
  393.1 1.0 copy-start
  557.5 0.7 copy-start.1
Sparse Core Ops, SparseCore 0:
  11.0 59.4 all-gather.5
  73.5 108.3 all-gather.7
  192.7 56.2 all-gather.9
  251.9 108.9 all-gather.11
  394.9 55.9 all-gather.13

commit v2 on v1

v2 whole, which is shorter than its diff:
```python
import jax
import jax.numpy as jnp
from jax import lax
from jax.sharding import PartitionSpec as P

BLK = 128
P_SIZE = 384
NFB = 16
NPB = 3


HIGH = lax.Precision.HIGHEST


def partner(array, axis, stride):
    return lax.ppermute(array, axis, [(i, i ^ 1 << stride) for i in range(lax.axis_size(axis))])


def gather_rows(array):
    return lax.all_gather(array, "fr", axis=0, tiled=True)


def dot_t(left, right):
    return jnp.dot(left, right.T, precision=HIGH, preferred_element_type=jnp.float32)


def factor(columns):
    trailing = columns
    panels = []
    for block_index in range(NPB):
        block_low = block_index * BLK
        lower_block = jnp.tril(jnp.linalg.cholesky(trailing[:BLK, :BLK]))
        below = lax.linalg.triangular_solve(
            lower_block, trailing[BLK:, :BLK], left_side=False, lower=True, transpose_a=True
        )
        panels.append(
            jnp.concatenate(
                [jnp.zeros((block_low, BLK), jnp.float32), lower_block, below], axis=0
            )
        )
        if block_index < NPB - 1:
            width = trailing.shape[1] - BLK
            trailing = trailing[BLK:, BLK:] - dot_t(below, below[:width])
    return jnp.concatenate(panels, axis=1)


def block_source(block_map):
    match = block_map[None, :] == jnp.arange(NFB, dtype=jnp.int32)[:, None]
    return jnp.any(match, axis=1), jnp.argmax(match, axis=1)


def extend_columns(rest, panel, block_map):
    has, source = block_source(block_map)
    lower = panel[P_SIZE:]
    count = NFB - NPB
    picked = jnp.take(rest[P_SIZE:].reshape(count * BLK, count, BLK), source[:NPB], axis=1)
    picked_panel = jnp.take(lower.reshape(count, BLK, P_SIZE), source[:NPB], axis=0)
    schur = picked.reshape(count * BLK, P_SIZE) - dot_t(lower, picked_panel.reshape(P_SIZE, P_SIZE))
    schur = jnp.where(jnp.repeat(has[:NPB], BLK)[None, :], schur, 0.0)
    rows = jnp.take(schur.reshape(count, BLK, P_SIZE), source, axis=0)
    rows = jnp.where(has[:, None, None], rows, 0.0)
    return rows.reshape(NFB * BLK, P_SIZE)


def extend_own(rest, panel, block_map):
    has, source = block_source(block_map)
    parent_block = lax.axis_index("fr")
    present = has[parent_block]
    child_block = NPB + source[parent_block]
    rows = lax.dynamic_slice_in_dim(rest, child_block * BLK, BLK, 0)
    panel_rows = lax.dynamic_slice_in_dim(panel, child_block * BLK, BLK, 0)
    schur = rows - dot_t(panel_rows, panel[P_SIZE:])
    tiles = schur.reshape(BLK, NFB - NPB, BLK)
    placed = jnp.take(tiles, source[NPB:], axis=1)
    placed = jnp.where(has[None, NPB:, None] & present, placed, 0.0)
    return placed.reshape(BLK, (NFB - NPB) * BLK)


def parent(rest, panel, block_map, shares_full, level_bit):
    columns = extend_columns(rest, panel, block_map)
    own_rest = extend_own(rest, panel, block_map)
    columns = shares_full + (columns + partner(columns, "sub", level_bit))
    own_rest = own_rest + partner(own_rest, "sub", level_bit)
    return columns, own_rest


def local(front_leaf, shares_one, shares_two, map_leaf, map_mid):
    row_count = front_leaf.shape[0]
    row_start = lax.axis_index("fr") * row_count
    sub_index = lax.axis_index("sub")

    one_own = shares_one + partner(shares_one, "sub", 0)
    two_own = shares_two + partner(shares_two, "sub", 0)
    two_own = two_own + partner(two_own, "sub", 1)

    leaf = front_leaf.astype(jnp.float32)
    leaf_full = factor(gather_rows(leaf[:, :P_SIZE]))
    leaf_rest = gather_rows(leaf[:, P_SIZE:])
    one_full = gather_rows(one_own)
    leaf_panel = lax.dynamic_slice_in_dim(leaf_full, row_start, row_count, 0)

    middle_columns, middle_own = parent(leaf_rest, leaf_full, map_leaf[0], one_full, 0)
    middle_full = factor(middle_columns)
    middle_rest = gather_rows(middle_own)
    two_full = gather_rows(two_own)
    middle_panel = lax.dynamic_slice_in_dim(middle_full, row_start, row_count, 0)

    pair_map = lax.dynamic_index_in_dim(map_mid, sub_index // 2, 0, keepdims=False)
    top_columns, top_own = parent(middle_rest, middle_full, pair_map, two_full, 1)
    top_full = factor(top_columns)
    top_panel = lax.dynamic_slice_in_dim(top_full, row_start, row_count, 0)

    schur = top_own - dot_t(top_panel, top_full[P_SIZE:])
    row_ids = row_start + jnp.arange(row_count)
    contribution = jnp.where((row_ids >= P_SIZE)[:, None], schur, 0.0)
    return (leaf_panel, middle_panel, top_panel, contribution)


def solution(mesh):
    in_specs = (
        P(("sub", "fr"), None),
        P(("sub", "fr"), None),
        P(("sub", "fr"), None),
        P("sub", None),
        P(),
    )
    out_specs = (
        P(("sub", "fr"), None),
        P(("sub", "fr"), None),
        P(("sub", "fr"), None),
        P(("sub", "fr"), None),
    )
    return jax.shard_map(local, mesh=mesh, in_specs=in_specs, out_specs=out_specs, check_vma=False)
```

time: 583 us -> 653 us (1.12)
  local copies, waits for them, and re-layouts: 39 us -> 147 us
  waiting for transfers between devices: 188 us -> 139 us
  matrix products: 44.1 us -> 67.7 us
  other arithmetic: 278 us -> 265 us
    all_gather x5, waiting for transfers between devices: 163 us -> 80.5 us  [gather_rows(): return lax.all_gather(array, 'fr', axis=0, tiled=True)]
    another operation x44 -> x47, other arithmetic: 263 us -> 212 us  [the longest x27 113 us: factor(): lower_block = jnp.tril(jnp.linalg.cholesky(trailing[:BLK, :BLK]))]
    slice x11 -> x27, local copies, waits for them, and re-layouts: 8.35 us -> 46.4 us  [the longest x3 31.2 us: extend_columns(): rest[P_SIZE:].reshape(count * BLK, count, BLK)]
    dot_general x3 -> x11, matrix products: 16.4 us -> 52.9 us  [dot_t(): jnp.dot(left, right.T, precision=HIGH, preferred_element_type=jnp.float32)]
    reshape x0 -> x9, local copies, waits for them, and re-layouts: none -> 35.6 us  [the longest x1 13.2 us: extend_columns(): rest[P_SIZE:].reshape(count * BLK, count, BLK)]
    ppermute x3 -> x7, waiting for transfers between devices: 24.9 us -> 58.4 us  [partner(): lax.ppermute(array, axis, [(i, i ^ 1 << stride) for i in range(lax.axis_s...]
    gather x2 -> x8, local copies, waits for them, and re-layouts: 1.23 us -> 32.7 us  [the longest x2 12.7 us: extend_columns(): jnp.take(rest[P_SIZE:].reshape(count * BLK, count, BLK), source[:NPB], ax...]
    select_n x4 -> x9, other arithmetic: 0.4 us -> 24.3 us  [the longest x2 8.43 us: extend_columns(): rows = jnp.where(has[:, None, None], rows, 0.0)]
  transfers between devices with their start and end apart: 8 -> 12, of which waited for: 7 -> 7; matrix products, arithmetic and copies ran while one was open for 41% -> 72% of each run, Pallas kernels for 0% -> 0%
where the time goes in v2:
time: 653 us; the launch traced here: 641 us
  other arithmetic  265 us (41%)
  local copies, waits for them, and re-layouts  147 us (23%)
  waiting for transfers between devices  139 us (21%)
  matrix products  67.7 us (10%)
  between operations  16.3 us (2%)
    another operation x27, other arithmetic, factor(): lower_block = jnp.tril(jnp.linalg.cholesky(trailing[:BLK, :BLK]))  113 us
    another operation x18, other arithmetic, factor(): lax.linalg.triangular_solve(lower_block, trailing[BLK:, :BLK], left_side=...  97.7 us
    all_gather x5, waiting for transfers between devices, gather_rows(): return lax.all_gather(array, 'fr', axis=0, tiled=True)  80.5 us
    ppermute x7, waiting for transfers between devices, partner(): lax.ppermute(array, axis, [(i, i ^ 1 << stride) for i in range(lax.axis_s...  58.4 us
    dot_general x11, matrix products, dot_t(): jnp.dot(left, right.T, precision=HIGH, preferred_element_type=jnp.float32)  52.9 us
    slice x3, local copies, waits for them, and re-layouts, extend_columns(): rest[P_SIZE:].reshape(count * BLK, count, BLK)  31.2 us
    unnamed x61, local copies, waits for them, and re-layouts  18.4 us
    another operation x9, matrix products, factor(): lax.linalg.triangular_solve(lower_block, trailing[BLK:, :BLK], left_side=...  14.8 us
  transfers between devices with their start and end apart: 12, of which 7 were waited for; matrix products, arithmetic and copies ran while one was open for 72% of the time, Pallas kernels for 0%

profile of v2, /device:TPU:2, one launch (start us, length us, event | category | flops | bytes accessed | tf_op | source)
XLA Modules:
  0.0 640.8 jit_solution(1613157285148802837)
XLA Ops:
  17.6 52.9 %all-gather.6.cloned.1.call-done = f32[2048,384]{0,1:T(8,128)} async-done(((f32[128,384]{0,1:T(8,128)}), f32[2048,384]{0,1:T(8,128)}) %all-gather.6.cloned.1.call-update) | async-done | bytes 3145744 | tf_op jit(solution)/shard_map/all_gather | solution.py:20
  72.3 11.7 %cholesky.149 = f32[128,128]{1,0:T(8,128)S(1)} custom-call(f32[128,128]{1,0:T(8,128)S(1)} %fusion.65), custom_call_target="Cholesky" | custom-call | tf_op jit(solution)/shard_map/jit(cholesky)/cholesky | solution.py:32
  85.4 9.8 %custom-call.17 = f32[1,128,128]{1,2,0:T(8,128)S(1)} custom-call(f32[1,128,128]{2,1,0:T(8,128)S(1)} %get-tuple-element.56), custom_call_target="InvertDiagBlocksLowerTriangular" | custom-call | tf_op jit(solution)/shard_map/triangular_solve/custom-call.0 | solution.py:33
  98.5 3.3 convolution_subtract_fusion.2
  101.9 12.0 %cholesky.160 = f32[128,128]{1,0:T(8,128)S(1)} custom-call(f32[128,128]{1,0:T(8,128)S(1)} %fusion.63), custom_call_target="Cholesky" | custom-call | tf_op jit(solution)/shard_map/jit(cholesky)/cholesky | solution.py:32
  115.3 9.8 %custom-call.18 = f32[1,128,128]{1,2,0:T(8,128)S(1)} custom-call(f32[1,128,128]{2,1,0:T(8,128)S(1)} %get-tuple-element.54), custom_call_target="InvertDiagBlocksLowerTriangular" | custom-call | tf_op jit(solution)/shard_map/triangular_solve/custom-call.2 | solution.py:33
  128.2 11.7 %cholesky.171 = f32[128,128]{1,0:T(8,128)S(1)} custom-call(f32[128,128]{1,0:T(8,128)S(1)} %fusion.61), custom_call_target="Cholesky" | custom-call | tf_op jit(solution)/shard_map/jit(cholesky)/cholesky | solution.py:32
  141.2 9.8 %custom-call.19 = f32[1,128,128]{1,2,0:T(8,128)S(1)} custom-call(f32[1,128,128]{2,1,0:T(8,128)S(1)} %get-tuple-element.52), custom_call_target="InvertDiagBlocksLowerTriangular" | custom-call | tf_op jit(solution)/shard_map/triangular_solve/custom-call.3 | solution.py:33
  154.3 27.6 %all-gather.10.cloned.1.call-done = f32[2048,1664]{0,1:T(8,128)} async-done(((f32[128,1664]{0,1:T(8,128)}), f32[2048,1664]{0,1:T(8,128)}) %all-gather.10.cloned.1.call-update) | async-done | bytes 13631504 | tf_op jit(solution)/shard_map/all_gather | solution.py:20
  182.0 6.5 %convolution_subtract_fusion.3 = f32[128,1664]{0,1:T(8,128)} fusion(f32[2048,1664]{0,1:T(8,128)} %all-gather.10.cloned.1.call-done, s32[]{:T(128)S(6)} %select_n.129, f32[2048,384]{0,1:T(8,128)S(1)} %fusion.2), kind=kOutput, calls=%fused_computation.38 | convolution fusion | flops 981680128 | bytes 4457472 | tf_op jit(solution)/shard_map/dot_general | solution.py:24
  208.2 3.4 copy.167
  216.8 9.0 %slice.222 = f32[1664,1664]{0,1:T(8,128)} slice(f32[2048,1664]{0,1:T(8,128)} %all-gather.10.cloned.1.call-done), slice={[384:2048], [0:1664]} | slice | bytes 22151168 | tf_op jit(solution)/shard_map/slice | solution.py:56
  225.8 6.4 %gather_fusion = f32[3,1664,128]{1,2,0:T(8,128)} fusion(f32[1664,13,128]{0,2,1:T(8,128)} %bitcast.146, s32[1024]{0:T(1024)S(1)} %pad_clamp_fusion.5), kind=kCustom, calls=%fused_computation.clone | custom fusion | bytes 5111820 | tf_op jit(solution)/shard_map/jit(_take)/gather | solution.py:56
  232.2 3.4 broadcast_select_fusion
  235.6 3.4 copy.168
  239.0 12.2 %fusion.13 = f32[1664,384]{1,0:T(8,128)} fusion(f32[1664,384]{1,0:T(8,128)} %copy.168, f32[384,384]{1,0:T(8,128)} %bitcast.160, pred[384]{0:T(512)(128)(4,1)S(1)} %broadcast_bitcast_fusion.1, f32[2048,384]{0,1:T(8,128)S(1)} %fusion.2), kind=kOutput, calls=%fused_computation.33 | convolution fusion | flops 2945679360 | bytes 8258048 | tf_op jit(solution)/shard_map/dot_general | solution.py:24
  251.2 4.1 gather_fusion.2
  255.3 4.4 select_select_fusion.1
  259.7 3.5 copy.216
  271.7 4.8 collective-permute-done.3
  277.2 4.7 add_add_fusion.1
  284.5 11.7 %cholesky.182 = f32[128,128]{1,0:T(8,128)S(1)} custom-call(f32[128,128]{1,0:T(8,128)S(1)} %fusion.59), custom_call_target="Cholesky" | custom-call | tf_op jit(solution)/shard_map/jit(cholesky)/cholesky | solution.py:32
  297.6 9.8 %custom-call.20 = f32[1,128,128]{1,2,0:T(8,128)S(1)} custom-call(f32[1,128,128]{2,1,0:T(8,128)S(1)} %get-tuple-element.48), custom_call_target="InvertDiagBlocksLowerTriangular" | custom-call | tf_op jit(solution)/shard_map/triangular_solve/custom-call.0 | solution.py:33
  310.5 3.3 slice_subtract_fusion.1
  316.1 11.9 %cholesky.193 = f32[128,128]{1,0:T(8,128)S(1)} custom-call(f32[128,128]{1,0:T(8,128)S(1)} %fusion.57), custom_call_target="Cholesky" | custom-call | tf_op jit(solution)/shard_map/jit(cholesky)/cholesky | solution.py:32
  329.9 10.6 %custom-call.21 = f32[1,128,128]{1,2,0:T(8,128)S(1)} custom-call(f32[1,128,128]{2,1,0:T(8,128)} %get-tuple-element.46), custom_call_target="InvertDiagBlocksLowerTriangular" | custom-call | tf_op jit(solution)/shard_map/triangular_solve/custom-call.2 | solution.py:33
  350.0 12.6 %cholesky.204 = f32[128,128]{1,0:T(8,128)S(1)} custom-call(f32[128,128]{1,0:T(8,128)} %fusion.55), custom_call_target="Cholesky" | custom-call | tf_op jit(solution)/shard_map/jit(cholesky)/cholesky | solution.py:32
  364.4 11.3 %custom-call.22 = f32[1,128,128]{1,2,0:T(8,128)} custom-call(f32[1,128,128]{2,1,0:T(8,128)} %get-tuple-element.44), custom_call_target="InvertDiagBlocksLowerTriangular" | custom-call | tf_op jit(solution)/shard_map/triangular_solve/custom-call.3 | solution.py:33
  392.7 8.9 %slice.234 = f32[1664,1664]{1,0:T(8,128)} slice(f32[2048,1664]{1,0:T(8,128)} %all-gather.14.cloned.1.call-done), slice={[384:2048], [0:1664]} | slice | bytes 22151168 | tf_op jit(solution)/shard_map/slice | solution.py:56
  401.6 13.3 %copy.186 = f32[1664,1664]{0,1:T(8,128)} copy(f32[1664,1664]{1,0:T(8,128)} %slice.234) | data formatting | bytes 22151168 | tf_op jit(solution)/shard_map/slice | solution.py:56
  414.9 13.2 %copy.187 = f32[1664,13,128]{2,0,1:T(8,128)} copy(f32[1664,13,128]{0,2,1:T(8,128)} %bitcast.145) | data formatting | bytes 22151168 | tf_op jit(solution)/shard_map/reshape | solution.py:56
  428.1 6.3 gather_fusion.4
  434.4 3.4 select_bitcast_fusion
  441.1 3.7 copy.190
  444.9 12.4 %fusion.12 = f32[1664,384]{1,0:T(8,128)} fusion(f32[1664,384]{1,0:T(8,128)} %copy.190, f32[384,384]{1,0:T(8,128)} %bitcast.159, pred[384]{0:T(512)(128)(4,1)S(1)} %copy-done.19, f32[2048,384]{0,1:T(8,128)} %copy-done.2), kind=kOutput, calls=%fused_computation.31 | convolution fusion | flops 2945679360 | bytes 8257920 | tf_op jit(solution)/shard_map/dot_general | solution.py:24
  457.2 4.1 gather_fusion.6
  461.4 4.0 select_select_fusion
  465.4 3.5 copy.217
  475.6 3.8 dynamic-slice_subtract_fusion
  491.4 48.9 %collective-permute-done.5 = f32[2048,384]{0,1:T(8,128)} collective-permute-done((f32[2048,384]{0,1:T(8,128)}, f32[2048,384]{0,1:T(8,128)}, u32[]{:S(2)}, u32[]{:S(2)}) %collective-permute-start.5) | collective-permute-done | bytes 3145760 | tf_op jit(solution)/shard_map/ppermute | solution.py:16
  540.2 3.9 add_add_fusion
  546.7 11.7 %cholesky.215 = f32[128,128]{1,0:T(8,128)S(1)} custom-call(f32[128,128]{1,0:T(8,128)S(1)} %fusion.53), custom_call_target="Cholesky" | custom-call | tf_op jit(solution)/shard_map/jit(cholesky)/cholesky | solution.py:32
  559.8 9.8 %custom-call.23 = f32[1,128,128]{1,2,0:T(8,128)S(1)} custom-call(f32[1,128,128]{2,1,0:T(8,128)S(1)} %get-tuple-element.38), custom_call_target="InvertDiagBlocksLowerTriangular" | custom-call | tf_op jit(solution)/shard_map/triangular_solve/custom-call.0 | solution.py:33
  576.3 11.9 %cholesky.226 = f32[128,128]{1,0:T(8,128)S(1)} custom-call(f32[128,128]{1,0:T(8,128)S(1)} %fusion.51), custom_call_target="Cholesky" | custom-call | tf_op jit(solution)/shard_map/jit(cholesky)/cholesky | solution.py:32
  589.6 9.8 %custom-call.24 = f32[1,128,128]{1,2,0:T(8,128)S(1)} custom-call(f32[1,128,128]{2,1,0:T(8,128)S(1)} %get-tuple-element.36), custom_call_target="InvertDiagBlocksLowerTriangular" | custom-call | tf_op jit(solution)/shard_map/triangular_solve/custom-call.2 | solution.py:33
  602.4 11.7 %cholesky.237 = f32[128,128]{1,0:T(8,128)S(1)} custom-call(f32[128,128]{1,0:T(8,128)S(1)} %fusion.49), custom_call_target="Cholesky" | custom-call | tf_op jit(solution)/shard_map/jit(cholesky)/cholesky | solution.py:32
  615.5 9.8 %custom-call.25 = f32[1,128,128]{1,2,0:T(8,128)S(1)} custom-call(f32[1,128,128]{2,1,0:T(8,128)S(1)} %get-tuple-element.34), custom_call_target="InvertDiagBlocksLowerTriangular" | custom-call | tf_op jit(solution)/shard_map/triangular_solve/custom-call.3 | solution.py:33
  629.7 4.1 subtract_select_fusion
  (220 shorter events, 140.5 us)
Async XLA Ops:
  7.2 4.5 copy-start
  7.2 4.2 copy-start.14
  7.2 5.2 copy-start.25
  7.2 63.3 %all-gather.6.cloned.1.call-start = ((), (), s32[]{:S(2)}) async-start(), calls=%async_computation | async-start | bytes 3342336 | tf_op jit(solution)/shard_map/all_gather | solution.py:20
  9.0 172.9 %all-gather.10.cloned.1.call-start = ((), (), s32[]{:S(2)}) async-start(), calls=%async_computation.2 | async-start | bytes 14483456 | tf_op jit(solution)/shard_map/all_gather | solution.py:20
  11.4 265.8 %all-gather.8.cloned.1.call-start = ((), (), s32[]{:S(2)}) async-start(), calls=%async_computation.1 | async-start | bytes 3342336 | tf_op jit(solution)/shard_map/all_gather | solution.py:20
  11.6 1.5 collective-permute-start
  11.7 83.6 %copy-start.26 = (s32[13]{0:T(128)}, s32[13]{0:T(128)S(1)}, u32[]{:S(2)}) copy-start(s32[13]{0:T(128)S(1)} %fusion.70) | copy-start | bytes 160
  13.8 378.9 %all-gather.14.cloned.1.call-start = ((), (), s32[]{:S(2)}) async-start(), calls=%async_computation.4 | async-start | bytes 14483456 | tf_op jit(solution)/shard_map/all_gather | solution.py:20
  14.0 56.5 %copy-start.23 = (pred[16]{0:T(512)(128)(4,1)}, pred[16]{0:T(512)(128)(4,1)S(1)}, u32[]{:S(2)}) copy-start(pred[16]{0:T(512)(128)(4,1)S(1)} %fusion.67) | copy-start | bytes 52
  97.5 1.0 copy-start.6
  126.2 0.9 copy-start.10
  154.3 39.1 %copy-start.15 = (pred[13]{0:T(512)(128)(4,1)S(1)}, pred[13]{0:T(512)(128)(4,1)}, u32[]{:S(2)}) copy-start(pred[13]{0:T(512)(128)(4,1)} %get-tuple-element.60) | copy-start | bytes 43
  154.3 39.1 %copy-start.20 = (pred[13]{0:T(512)(128)(4,1)S(1)}, pred[13]{0:T(512)(128)(4,1)}, u32[]{:S(2)}) copy-start(pred[13]{0:T(512)(128)(4,1)} %slice_and_fusion.1) | copy-start | bytes 43
  195.7 10.2 %copy-start.24 = (pred[16]{0:T(512)(128)(4,1)S(1)}, pred[16]{0:T(512)(128)(4,1)}, u32[]{:S(2)}) copy-start(pred[16]{0:T(512)(128)(4,1)} %copy-done.23) | copy-start | bytes 52
  200.4 2.6 collective-permute-start.4
  205.3 286.1 %all-gather.12.cloned.1.call-start = ((), (), s32[]{:S(2)}) async-start(), calls=%async_computation.3 | async-start | bytes 3342336 | tf_op jit(solution)/shard_map/all_gather | solution.py:20
  263.2 14.0 %collective-permute-start.1 = (f32[2048,384]{0,1:T(8,128)}, f32[2048,384]{0,1:T(8,128)}, u32[]{:S(2)}, u32[]{:S(2)}) collective-permute-start(f32[2048,384]{0,1:T(8,128)} %copy.216), channel_id=1, source_target_pairs={{0,16},{16,0},{32,48},{48,32},{64,80},{80,64},{96,112},{112,96},{1... | collective-permute-start | bytes 9437192 | tf_op jit(solution)/shard_map/ppermute | solution.py:16
  264.4 4.9 collective-permute-start.2
  267.3 9.2 %copy-start.21 = (pred[16]{0:T(512)(128)(4,1)}, pred[16]{0:T(512)(128)(4,1)S(1)}, u32[]{:S(2)}) copy-start(pred[16]{0:T(512)(128)(4,1)S(1)} %fusion.66) | copy-start | bytes 52
  269.4 7.1 %collective-permute-start.3 = (f32[128,384]{0,1:T(8,128)S(1)}, f32[128,384]{0,1:T(8,128)S(1)}, u32[]{:S(2)}, u32[]{:S(2)}) collective-permute-start(f32[128,384]{0,1:T(8,128)S(1)} %add.95), channel_id=1, source_target_pairs={{0,32},{16,48},{32,0},{48,16},{64,96},{80,112},{96,64},{112,80},{1... | collective-permute-start | bytes 589832 | tf_op jit(solution)/shard_map/ppermute | solution.py:16
  281.9 1.6 copy-start.5
  309.6 1.0 copy-start.7
  313.9 1.3 copy-start.12
  342.7 1.0 copy-start.9
  345.8 0.9 copy-start.13
  380.9 1.6 copy-start.2
  384.2 6.4 %copy-start.17 = (pred[3]{0:T(512)(128)(4,1)S(1)}, pred[3]{0:T(512)(128)(4,1)}, u32[]{:S(2)}) copy-start(pred[3]{0:T(512)(128)(4,1)} %get-tuple-element.40) | copy-start | bytes 13
  441.1 3.7 copy-start.19
  457.2 4.1 copy-start.18
  457.2 4.1 copy-start.22
  465.4 6.9 %copy-start.16 = (s32[13]{0:T(128)S(1)}, s32[13]{0:T(128)}, u32[]{:S(2)}) copy-start(s32[13]{0:T(128)} %get-tuple-element.33) | copy-start | bytes 160
  468.9 71.3 %collective-permute-start.5 = (f32[2048,384]{0,1:T(8,128)}, f32[2048,384]{0,1:T(8,128)}, u32[]{:S(2)}, u32[]{:S(2)}) collective-permute-start(f32[2048,384]{0,1:T(8,128)} %copy.217), channel_id=1, source_target_pairs={{0,32},{16,48},{32,0},{48,16},{64,96},{80,112},{96,64},{112,80},{1... | collective-permute-start | bytes 9437192 | tf_op jit(solution)/shard_map/ppermute | solution.py:16
  481.0 59.3 %copy-start.3 = (f32[2048,384]{0,1:T(8,128)S(1)}, f32[2048,384]{0,1:T(8,128)}, u32[]{:S(2)}) copy-start(f32[2048,384]{0,1:T(8,128)} %copy.217) | copy-start | bytes 9437188
  490.7 138.9 %collective-permute-start.6 = (f32[128,1664]{1,0:T(8,128)}, f32[128,1664]{1,0:T(8,128)}, u32[]{:S(2)}, u32[]{:S(2)}) collective-permute-start(f32[128,1664]{1,0:T(8,128)} %copy.205), channel_id=1, source_target_pairs={{0,32},{16,48},{32,0},{48,16},{64,96},{80,112},{96,64},{112,80},{1... | collective-permute-start | bytes 2555912 | tf_op jit(solution)/shard_map/ppermute | solution.py:16
  544.1 1.7 copy-start.4
  571.9 1.0 copy-start.8
  600.4 0.9 copy-start.11
  626.6 7.2 %copy-start.1 = (s32[8,13]{1,0:T(8,128)S(1)}, s32[8,13]{1,0:T(8,128)}, u32[]{:S(2)}) copy-start(s32[8,13]{1,0:T(8,128)} %param.24) | copy-start | bytes 1252
Sparse Core Ops, SparseCore 0:
  11.0 59.4 all-gather.5
  73.5 108.4 all-gather.9
  184.9 56.2 all-gather.7
  244.1 99.8 all-gather.13
  346.8 56.3 all-gather.11
